TPU v7x, 256 devices: a whole 4x4x8 slice. The times are simulated.
256 devices in a mesh: kv: 8 (over z), blk: 32 (over y, x, core).
Axes of the slice: x: 4, y: 4, z: 8, core: 2. Of those that a mesh axis runs over, the one named last changes fastest.
Arguments:
- hidden_in: bfloat16 [4, 16, 4096], P(None, None, 'blk'), may hold values from -6 to 6
- attn_gain: bfloat16 [4096], P('blk'), may hold values from 0.5 to 1.5
- ffn_gain: bfloat16 [4096], replicated, may hold values from 0.5 to 1.5
- query_key_value_weight: bfloat16 [4096, 8, 768], P('blk', 'kv'), may hold values from -0.09375 to 0.09375
- out_weight: bfloat16 [4096, 4096], P('kv', 'blk'), may hold values from -0.09375 to 0.09375
- router_weight: bfloat16 [4096, 8], replicated, may hold values from -0.09375 to 0.09375
- expert_in: bfloat16 [8, 4096, 2, 8192], P('kv', None, None, 'blk'), may hold values from -0.09375 to 0.09375
- expert_down: bfloat16 [8, 8192, 4096], P('kv', 'blk'), may hold values from -0.125 to 0.125
- kv_cache: bfloat16 [2048, 2, 8, 128, 128], P('blk', None, 'kv')
- lengths: int32 [2], replicated, may hold values from 1 to 16384, as said below
- tables: int32 [16, 128], replicated, may hold values from 0 to 2047, as said below
- parents: int32 [4, 16], replicated, may hold values from 0 to 15, as said below
- routes: int32 [4, 16, 2], replicated, may hold values from 0 to 7, all different within a row; in each aligned block of 16 rows (0 to 15, 16 to 31, ..., all dimensions but the last counted through in order) at most 6 rows name the same one
Outputs:
- layer_out: bfloat16 [4, 16, 4096], P(None, None, 'blk')
Inputs may be any that keep to these rules, and one draw needn't show every extreme that they name: `lengths`: one group has exactly 16384 cached positions. `tables`: each pool block is named exactly once. `parents`: a beam's parent is a beam of its own group of 8 consecutive beams. `routes`: in each step no expert is named by more than 6 beams, a bound that some block reaches.
All inputs are finite; a program needn't handle non-finite values.
Results may differ from a plain program's by a relative error of at most 0.013.
Values may be sent and summed in bfloat16 or wider, within the bound.
No kernel may reach another device: no remote copies, remote signals or barrier semaphores. Data moves between devices by JAX's collectives and lax.ppermute only.
A program may use at most 64 MiB of HBM per device.

v0:
```python
import math
import jax
import jax.numpy as jnp
from jax import lax
from jax.sharding import PartitionSpec as P

MODEL_WIDTH = 4096
HEAD_WIDTH = 128
QUERIES_PER_KEY = 4
EXPERTS = 8
BEAM_W = 8
GROUPS = 2
DECODE_STEPS = 4
BLOCK_POSITIONS = 128
BEAM_BLOCKS = 128
BEAM_TOTAL = 16
CAP = 6
NORM_FLOOR = 1e-05
ROPE_BASE = 1000000.0
NEG_FILL = -1e30


def joined(value, axis, join):
    pieces = jax.tree.map(lambda part: lax.all_gather(part, axis), value)
    head = jax.tree.map(lambda part: part[0], pieces)
    tail = jax.tree.map(lambda part: part[1:], pieces)
    running, _ = lax.scan(lambda running, section: (join(running, section), None), head, tail)
    return running


def rotate_pairs(vectors, positions):
    half_width = vectors.shape[-1] // 2
    exponents = jnp.arange(half_width, dtype=jnp.float32) * (2.0 / vectors.shape[-1])
    frequency = ROPE_BASE ** (-exponents)
    angles = positions.astype(jnp.float32)[..., None] * frequency
    cosine = jnp.cos(angles)
    sine_part = jnp.sin(angles)
    lower_half = vectors[..., :half_width]
    upper_half = vectors[..., half_width:]
    return jnp.concatenate(
        [
            lower_half * cosine - upper_half * sine_part,
            upper_half * cosine + lower_half * sine_part,
        ],
        axis=-1,
    )


def lineage(parents):
    steps_count, beam_count = parents.shape
    beam_ids = jnp.arange(beam_count, dtype=jnp.int32)
    line_rows = []
    anchor_rows = []
    for step_index in range(steps_count):
        current = beam_ids
        levels = [jnp.full((beam_count,), -1, jnp.int32) for level_index in range(steps_count)]
        for level_index in range(step_index, -1, -1):
            levels[level_index] = current
            current = parents[level_index][current]
        line_rows.append(jnp.stack(levels))
        anchor_rows.append(current)
    return (jnp.stack(line_rows), jnp.stack(anchor_rows))


def expert_rank(routes):
    steps_count, beam_count, pick_count = routes.shape
    onehot = (routes[..., None] == jnp.arange(EXPERTS, dtype=jnp.int32)).astype(jnp.int32)
    flat_hits = onehot.reshape(steps_count, beam_count * pick_count, EXPERTS)
    before = jnp.cumsum(flat_hits, axis=1) - flat_hits
    return jnp.sum(before * flat_hits, axis=-1).reshape(steps_count, beam_count, pick_count)


def head_total(partial_value):
    return lax.psum(partial_value, "kv")


def combine_parts(part_one, part_two):
    max_one, sum_one, vector_one = part_one
    max_two, sum_two, vector_two = part_two
    larger = jnp.maximum(max_one, max_two)
    scale_one = jnp.exp(max_one - larger)
    scale_two = jnp.exp(max_two - larger)
    return (
        larger,
        sum_one * scale_one + sum_two * scale_two,
        vector_one * scale_one[..., None] + vector_two * scale_two[..., None],
    )


def groups_to_beams(grouped):
    shaped = grouped.reshape((GROUPS, DECODE_STEPS, BEAM_W, QUERIES_PER_KEY) + grouped.shape[2:])
    shaped = jnp.moveaxis(shaped, 1, 0)
    return shaped.reshape((DECODE_STEPS, BEAM_TOTAL, QUERIES_PER_KEY) + grouped.shape[2:])


def body(
    hidden_in,
    attn_gain,
    ffn_gain,
    query_key_value_weight,
    out_weight,
    router_weight,
    expert_in,
    expert_down,
    kv_cache,
    lengths,
    tables,
    parents,
    routes,
):
    count_tokens = DECODE_STEPS * BEAM_TOTAL
    width_local = hidden_in.shape[2]
    heads_local = query_key_value_weight.shape[1]
    logit_scale = 1.0 / math.sqrt(HEAD_WIDTH)
    line_beams, anchor = lineage(parents)
    flat_in = hidden_in.reshape(count_tokens, width_local).astype(jnp.float32)
    pre_attn = (flat_in * attn_gain.astype(jnp.float32)).astype(jnp.bfloat16)
    partial_proj = jnp.dot(
        pre_attn,
        query_key_value_weight.reshape(width_local, -1),
        preferred_element_type=jnp.float32,
    )
    partial_sq = jnp.sum(flat_in * flat_in, axis=1)
    projected_rows, square_sum = lax.psum((partial_proj, partial_sq), "blk")
    projected_rows = (
        projected_rows * lax.rsqrt(square_sum / MODEL_WIDTH + NORM_FLOOR)[:, None]
    ).reshape(DECODE_STEPS, BEAM_TOTAL, heads_local, QUERIES_PER_KEY + 2, HEAD_WIDTH)
    beam_groups = jnp.arange(BEAM_TOTAL, dtype=jnp.int32) // BEAM_W
    positions = lengths[beam_groups][None, :] + jnp.arange(DECODE_STEPS, dtype=jnp.int32)[:, None]
    queries = rotate_pairs(
        projected_rows[:, :, :, :QUERIES_PER_KEY], positions[:, :, None, None]
    ).astype(jnp.bfloat16)
    new_key = rotate_pairs(projected_rows[:, :, :, QUERIES_PER_KEY], positions[:, :, None]).astype(
        jnp.bfloat16
    )
    new_value = projected_rows[:, :, :, QUERIES_PER_KEY + 1].astype(jnp.bfloat16)
    slot_count = kv_cache.shape[0]
    slot_base = lax.axis_index("blk") * slot_count
    entry_ids = jnp.arange(BEAM_TOTAL * BEAM_BLOCKS, dtype=jnp.int32)
    owner_all = (
        jnp.zeros((BEAM_TOTAL * BEAM_BLOCKS,), jnp.int32)
        .at[tables.reshape(-1)]
        .set(entry_ids // BEAM_BLOCKS)
    )
    block_all = (
        jnp.zeros((BEAM_TOTAL * BEAM_BLOCKS,), jnp.int32)
        .at[tables.reshape(-1)]
        .set(entry_ids % BEAM_BLOCKS)
    )
    owner_here = lax.dynamic_slice_in_dim(owner_all, slot_base, slot_count)
    block_here = lax.dynamic_slice_in_dim(block_all, slot_base, slot_count)
    group_here = owner_here // BEAM_W
    live_keys = (
        block_here[:, None] * BLOCK_POSITIONS
        + jnp.arange(BLOCK_POSITIONS, dtype=jnp.int32)[None, :]
        < lengths[group_here][:, None]
    )
    anchor_groups = jnp.moveaxis(anchor.reshape(DECODE_STEPS, GROUPS, BEAM_W), 1, 0)
    anchor_query = jnp.broadcast_to(
        anchor_groups[..., None], (GROUPS, DECODE_STEPS, BEAM_W, QUERIES_PER_KEY)
    ).reshape(GROUPS, -1)
    query_match = anchor_query[group_here] == owner_here[:, None]
    group_hits = group_here[:, None] == jnp.arange(GROUPS, dtype=jnp.int32)[None, :]
    group_float = group_hits.astype(jnp.float32)
    recent_allowed = jnp.transpose(
        line_beams[:, :, :, None] == jnp.arange(BEAM_TOTAL, dtype=jnp.int32), (0, 2, 1, 3)
    ).reshape(DECODE_STEPS, BEAM_TOTAL, 1, count_tokens)
    is_first = lax.axis_index("blk") == 0
    query_head = queries[:, :, 0]
    query_groups = jnp.moveaxis(
        query_head.reshape(DECODE_STEPS, GROUPS, BEAM_W, QUERIES_PER_KEY, HEAD_WIDTH), 1, 0
    ).reshape(GROUPS, -1, HEAD_WIDTH)
    query_slots = query_groups[group_here]
    key_matrix = kv_cache[:, 0, 0]
    value_matrix = kv_cache[:, 1, 0]
    scores = (
        jnp.einsum("ptd,pqd->ptq", key_matrix, query_slots, preferred_element_type=jnp.float32)
        * logit_scale
    )
    allowed = live_keys[:, :, None] & query_match[:, None, :]
    masked = jnp.where(allowed, scores, NEG_FILL)
    slot_max = jnp.max(masked, axis=1)
    weights = jnp.where(allowed, jnp.exp(masked - slot_max[:, None, :]), 0.0)
    slot_sum = jnp.sum(weights, axis=1)
    slot_vector = jnp.einsum(
        "ptq,ptd->pqd",
        weights.astype(jnp.bfloat16),
        value_matrix,
        preferred_element_type=jnp.float32,
    )
    group_max = jnp.max(jnp.where(group_hits[:, :, None], slot_max[:, None, :], NEG_FILL), axis=0)
    rescale = jnp.exp(slot_max - group_max[group_here])
    group_sum = jnp.einsum(
        "pg,pq->gq", group_float, slot_sum * rescale, precision=lax.Precision.HIGHEST
    )
    group_vector = jnp.einsum(
        "pg,pqd->gqd",
        group_float,
        slot_vector * rescale[:, :, None],
        precision=lax.Precision.HIGHEST,
    )
    cache_max = groups_to_beams(group_max)
    cache_sum = groups_to_beams(group_sum)
    cache_vector = groups_to_beams(group_vector)
    newest_keys = new_key[:, :, 0].reshape(count_tokens, HEAD_WIDTH)
    newest_values = new_value[:, :, 0].reshape(count_tokens, HEAD_WIDTH)
    newest_logits = (
        jnp.einsum("sbqd,kd->sbqk", query_head, newest_keys, preferred_element_type=jnp.float32)
        * logit_scale
    )
    recent_masked = jnp.where(recent_allowed, newest_logits, NEG_FILL)
    recent_max = jnp.max(recent_masked, axis=-1)
    recent_weights = jnp.where(recent_allowed, jnp.exp(recent_masked - recent_max[..., None]), 0.0)
    recent_sum = jnp.sum(recent_weights, axis=-1)
    recent_vector = jnp.einsum(
        "sbqk,kd->sbqd",
        recent_weights.astype(jnp.bfloat16),
        newest_values,
        preferred_element_type=jnp.float32,
    )
    recent_max = jnp.where(is_first, recent_max, NEG_FILL)
    recent_sum = jnp.where(is_first, recent_sum, 0.0)
    recent_vector = jnp.where(is_first, recent_vector, 0.0)
    local_max, local_sum, local_vector = combine_parts(
        (cache_max, cache_sum, cache_vector), (recent_max, recent_sum, recent_vector)
    )
    max_heads = [local_max]
    sum_heads = [local_sum]
    vector_heads = [local_vector]
    part_max = jnp.stack(max_heads, axis=2)
    part_sum = jnp.stack(sum_heads, axis=2)
    part_vector = jnp.stack(vector_heads, axis=2)
    whole_max, whole_sum, whole_vector = joined(
        (part_max, part_sum, part_vector), "blk", combine_parts
    )
    attended_rows = (
        (whole_vector / whole_sum[..., None]).astype(jnp.bfloat16).reshape(count_tokens, -1)
    )
    attn_partial = jnp.dot(attended_rows, out_weight, preferred_element_type=jnp.float32)
    attn_out = head_total(attn_partial)
    residual = (flat_in + attn_out).astype(jnp.bfloat16)
    experts_local = expert_in.shape[0]
    ff_local = expert_in.shape[3]
    rows_per_expert = DECODE_STEPS * CAP
    rows_local = experts_local * rows_per_expert
    flat_routes = routes.reshape(count_tokens, 2)
    rank = expert_rank(routes).reshape(count_tokens, 2)
    step_of = jnp.arange(count_tokens, dtype=jnp.int32) // BEAM_TOTAL
    row_id = (flat_routes * rows_per_expert + step_of[:, None] * CAP + rank).reshape(-1)
    token_ids = jnp.broadcast_to(
        jnp.arange(count_tokens, dtype=jnp.int32)[:, None], (count_tokens, 2)
    ).reshape(-1)
    table_size = EXPERTS * rows_per_expert
    row_token_all = jnp.zeros((table_size,), jnp.int32).at[row_id].set(token_ids)
    row_live_all = jnp.zeros((table_size,), jnp.float32).at[row_id].set(1.0)
    row_other_all = (
        jnp.zeros((table_size,), jnp.int32).at[row_id].set(flat_routes[:, ::-1].reshape(-1))
    )
    row_start = lax.axis_index("kv") * rows_local
    row_token = lax.dynamic_slice_in_dim(row_token_all, row_start, rows_local)
    row_live = lax.dynamic_slice_in_dim(row_live_all, row_start, rows_local)
    row_other = lax.dynamic_slice_in_dim(row_other_all, row_start, rows_local)
    row_own = (row_start + jnp.arange(rows_local, dtype=jnp.int32)) // rows_per_expert
    in_flat = expert_in.reshape(experts_local, MODEL_WIDTH, 2 * ff_local)
    gain_wide = ffn_gain.astype(jnp.float32)
    full_rows = lax.all_gather(residual, "blk", axis=1, tiled=True)
    chosen = full_rows[row_token].astype(jnp.float32)
    pre_rows = (chosen * gain_wide).astype(jnp.bfloat16)
    sums_in = jnp.einsum(
        "erd,edf->erf",
        pre_rows.reshape(experts_local, rows_per_expert, MODEL_WIDTH),
        in_flat,
        preferred_element_type=jnp.float32,
    )
    sums_router = jnp.dot(pre_rows, router_weight, preferred_element_type=jnp.float32)
    sum_sq = jnp.sum(chosen * chosen, axis=1)
    inv_rows = lax.rsqrt(sum_sq / MODEL_WIDTH + NORM_FLOOR)
    expert_act = sums_in * inv_rows.reshape(experts_local, rows_per_expert)[:, :, None]
    expert_hidden = (jax.nn.silu(expert_act[..., :ff_local]) * expert_act[..., ff_local:]).astype(
        jnp.bfloat16
    )
    down_part = jnp.einsum(
        "erf,efd->erd", expert_hidden, expert_down, preferred_element_type=jnp.float32
    ).reshape(rows_local, MODEL_WIDTH)
    expert_result = lax.psum_scatter(down_part, "blk", scatter_dimension=1, tiled=True)
    logits = sums_router * inv_rows[:, None]
    expert_ids = jnp.arange(EXPERTS, dtype=jnp.int32)
    own_logit = jnp.sum(jnp.where(row_own[:, None] == expert_ids[None, :], logits, 0.0), axis=1)
    other_logit = jnp.sum(jnp.where(row_other[:, None] == expert_ids[None, :], logits, 0.0), axis=1)
    gate_share = row_live / (1.0 + jnp.exp(other_logit - own_logit))
    weighted_values = expert_result * gate_share[:, None]
    placement = (row_token[None, :] == jnp.arange(count_tokens, dtype=jnp.int32)[:, None]).astype(
        jnp.float32
    )
    mixture_part = jnp.dot(placement, weighted_values, precision=lax.Precision.HIGHEST)
    mixture = head_total(mixture_part)
    layer_out = (residual.astype(jnp.float32) + mixture).astype(jnp.bfloat16)
    return layer_out.reshape(DECODE_STEPS, BEAM_TOTAL, width_local)


def solution(mesh):
    placed = (
        P(None, None, "blk"),
        P("blk"),
        P(),
        P("blk", "kv", None),
        P("kv", "blk"),
        P(),
        P("kv", None, None, "blk"),
        P("kv", "blk", None),
        P("blk", None, "kv", None, None),
        P(),
        P(),
        P(),
        P(),
    )
    return jax.shard_map(
        body, mesh=mesh, in_specs=placed, out_specs=P(None, None, "blk"), check_vma=False
    )
```

profile of v0, /device:TPU:2, one launch (start us, length us, event | category | flops | bytes accessed | tf_op | source)
XLA Modules:
  0.0 434.0 jit_solution(2719535748926274330)
XLA Ops:
  7.3 0.8 multiply_reduce_fusion
  8.2 1.8 fusion.31
  10.0 1.3 fusion.108
  12.1 8.0 %scatter_custom_fusion = s32[2048]{0:T(1024)S(1)} fusion(s32[2048]{0:T(1024)S(1)} %bitcast.249, s32[2048]{0:T(1024)S(1)} %add_select_fusion, s32[]{:T(128)} %constant.125.clone.1), kind=kCustom, calls=%fused_computation.168 | custom fusion | bytes 8196 | tf_op jit(solution)/shard_map/scatter | solution.py:143
  20.1 8.0 %scatter_custom_fusion.1 = s32[2048]{0:T(1024)S(1)} fusion(s32[2048]{0:T(1024)S(1)} %bitcast.250, s32[2048]{0:T(1024)S(1)} %fusion.64, s32[]{:T(128)} %constant.125.clone.1), kind=kCustom, calls=%fused_computation.166 | custom fusion | bytes 8196 | tf_op jit(solution)/shard_map/scatter | solution.py:148
  28.2 1.3 fusion.86
  29.5 1.4 compare_select_fusion.12
  31.0 0.8 slice_bitcast_fusion.5
  39.1 62.3 %psum.29 = f32[64]{0:T(128)S(1)} all-reduce(f32[64]{0:T(128)S(1)} %reduce_sum.66), channel_id=1, replica_groups=mesh['kv'=8,'blk'=32] {'blk'}, use_global_device_ids=true, to_apply=%region_4.5 | all-reduce | flops 64 | bytes 512 | tf_op jit(solution)/shard_map/psum | solution.py:124
  103.0 21.4 %all-reduce.2.cloned.1.call-done = f32[64,768]{1,0:T(8,128)} async-done(((f32[64,768]{1,0:T(8,128)}), f32[64,768]{1,0:T(8,128)}) %all-reduce.2.cloned.1.call-update) | async-done | bytes 196624 | tf_op jit(solution)/shard_map/psum | solution.py:124
  124.4 1.0 broadcast_multiply_fusion
  125.9 2.2 gather_fusion.11
  128.0 4.6 %fusion.8 = (f32[64,128]{1,0:T(8,128)S(1)}, f32[64,128,128]{1,2,0:T(8,128)}) fusion(pred[64,128]{1,0:T(8,128)(4,1)S(1)} %broadcast_compare_fusion.1, pred[64,128]{1,0:T(8,128)(4,1)S(1)} %add_compare_fusion, bf16[64,128,128]{2,1,0:T(8,128)(2,1)} %gather_fusion.11, bf16[64,2,1,128,128]{4,3,2,1,0:T(8,128)(2,1)} %param.23), kind=kOutput, calls=%fused_computation.35 | convolution fusion | flops 272621568 | bytes 8437760 | tf_op jit(solution)/shard_map/ptd,pqd->ptq/dot_general | solution.py:177
  133.9 5.8 %convolution_multiply_fusion = f32[64,128,128]{2,1,0:T(8,128)S(1)} fusion(f32[64,128,128]{1,2,0:T(8,128)} %get-tuple-element.131, f32[64,128]{1,0:T(8,128)S(1)} %subtract_exponential_fusion.1, bf16[64,2,1,128,128]{4,3,2,1,0:T(8,128)(2,1)} %param.23, f32[64,128]{1,0:T(8,128)S(1)} %get-tuple-element.130, pred[64,128]{1,0:T(8,128)(4,1)S(1)} %broadcast_compare_fusion.1, ...), kind=kOutput, calls=%fused_computation.38 | convolution fusion | flops 275775488 | bytes 10567680 | tf_op jit(solution)/shard_map/ptq,ptd->pqd/dot_general | solution.py:185
  139.8 3.8 fusion.6
  143.9 0.9 fusion.26
  146.4 4.9 %copy.153 = bf16[512,8,2,256]{3,1,2,0:T(8,128)(2,1)} copy(bf16[512,8,2,256]{3,2,1,0:T(2,128)(2,1)} %bitcast.232) | data formatting | bytes 8388608
  151.2 1.0 scatter_custom_fusion.2
  152.4 3.8 fusion.10
  157.0 22.3 %all_gather.13 = f32[32,4,16,1,4]{2,4,3,1,0:T(4,128)S(1)} all-gather(f32[1,4,16,1,4]{2,4,3,1,0:T(4,128)S(1)} %get-tuple-element.113), channel_id=1, replica_groups=mesh['kv'=8,'blk'=32] {'blk'}, dimensions={0}, use_global_device_ids=true | all-gather | bytes 33792 | tf_op jit(solution)/shard_map/all_gather | solution.py:24
  179.3 24.4 %all_gather.12 = f32[32,4,16,1,4]{2,4,3,1,0:T(4,128)S(1)} all-gather(f32[1,4,16,1,4]{2,4,3,1,0:T(4,128)S(1)} %get-tuple-element.114), channel_id=1, replica_groups=mesh['kv'=8,'blk'=32] {'blk'}, dimensions={0}, use_global_device_ids=true | all-gather | bytes 33792 | tf_op jit(solution)/shard_map/all_gather | solution.py:24
  203.8 0.9 slice_bitcast_fusion.2
  204.7 4.7 %slice.137 = f32[124,16,4,128]{3,1,2,0:T(8,128)} slice(f32[128,16,4,128]{3,1,2,0:T(8,128)} %all-gather.3.cloned.1.call-done), slice={[4:128], [0:16], [0:4], [0:128]} | slice | bytes 8126464 | tf_op jit(solution)/shard_map/slice | solution.py:26
  209.4 50.2 %while.14 = (s32[]{:T(128)}, f32[4,16,1,4]{1,3,2,0:T(4,128)S(1)}, f32[4,16,1,4]{1,3,2,0:T(4,128)S(1)}, f32[4,16,1,4,128]{4,3,2,1,0:T(4,128)S(1)}, f32[31,4,16,1,...) while((s32[]{:T(128)}, f32[4,16,1,4]{1,3,2,0:T(4,128)S(1)}, ...), condition=%wide.region_11.12_spmd, body=%wide.region_10.11_spmd.sunk | while | flops 100098 | bytes 674921 | solution.py:27
  209.7 0.9 constant_dynamic-slice_fusion.2
  211.3 0.9 constant_dynamic-slice_fusion.2
  212.9 0.9 constant_dynamic-slice_fusion.2
  214.5 0.9 constant_dynamic-slice_fusion.2
  216.1 0.9 constant_dynamic-slice_fusion.2
  217.8 0.9 constant_dynamic-slice_fusion.2
  219.4 0.9 constant_dynamic-slice_fusion.2
  221.0 0.9 constant_dynamic-slice_fusion.2
  222.6 0.9 constant_dynamic-slice_fusion.2
  224.2 0.9 constant_dynamic-slice_fusion.2
  225.9 0.9 constant_dynamic-slice_fusion.2
  227.5 0.9 constant_dynamic-slice_fusion.2
  229.1 0.9 constant_dynamic-slice_fusion.2
  230.7 0.9 constant_dynamic-slice_fusion.2
  232.3 0.9 constant_dynamic-slice_fusion.2
  233.9 0.9 constant_dynamic-slice_fusion.2
  235.6 0.9 constant_dynamic-slice_fusion.2
  237.2 0.9 constant_dynamic-slice_fusion.2
  238.8 0.9 constant_dynamic-slice_fusion.2
  240.4 0.9 constant_dynamic-slice_fusion.2
  242.0 0.9 constant_dynamic-slice_fusion.2
  243.7 0.9 constant_dynamic-slice_fusion.2
  245.3 0.9 constant_dynamic-slice_fusion.2
  246.9 0.9 constant_dynamic-slice_fusion.2
  248.5 0.9 constant_dynamic-slice_fusion.2
  250.1 0.9 constant_dynamic-slice_fusion.2
  251.8 0.9 constant_dynamic-slice_fusion.2
  253.4 0.9 constant_dynamic-slice_fusion.2
  255.0 0.9 constant_dynamic-slice_fusion.2
  256.6 0.9 constant_dynamic-slice_fusion.2
  258.2 0.9 constant_dynamic-slice_fusion.2
  260.0 30.2 %psum.30 = f32[64,128]{1,0:T(8,128)S(1)} all-reduce(f32[64,128]{1,0:T(8,128)S(1)} %fusion.38), channel_id=1, replica_groups=mesh['kv'=8,'blk'=32] {'kv'}, use_global_device_ids=true, to_apply=%region_12.13 | all-reduce | flops 8192 | bytes 65536 | tf_op jit(solution)/shard_map/psum | solution.py:74
  290.2 22.5 %all_gather.15 = bf16[64,4096]{1,0:T(8,128)(2,1)S(1)} all-gather(bf16[64,128]{1,0:T(8,128)(2,1)S(1)} %fusion.56), channel_id=1, replica_groups=mesh['kv'=8,'blk'=32] {'blk'}, dimensions={1}, use_global_device_ids=true | all-gather | bytes 540672 | tf_op jit(solution)/shard_map/all_gather | solution.py:266
  313.6 2.8 fusion.28
  316.5 1.1 fusion.15
  318.0 1.0 scatter_custom_fusion.4
  319.1 1.0 scatter_custom_fusion.3
  320.3 75.3 %reduce-scatter.2.cloned.1.call-done = f32[24,128]{1,0:T(8,128)} async-done(((f32[24,4096]{1,0:T(8,128)}), f32[24,128]{1,0:T(8,128)}) %reduce-scatter.2.cloned.1.call-update) | async-done | bytes 12304 | tf_op jit(solution)/shard_map/reduce_scatter | solution.py:285
  395.7 0.9 fusion.59
  396.6 30.2 %psum.31 = f32[64,128]{1,0:T(8,128)S(1)} all-reduce(f32[64,128]{1,0:T(8,128)S(1)} %fusion.59), channel_id=1, replica_groups=mesh['kv'=8,'blk'=32] {'kv'}, use_global_device_ids=true, to_apply=%region_22.23 | all-reduce | flops 8192 | bytes 65536 | tf_op jit(solution)/shard_map/psum | solution.py:74
  (333 shorter events, 38.4 us)
Async XLA Ops:
  6.5 309.9 %copy-start = (bf16[1,256,4096]{2,1,0:T(8,128)(2,1)S(1)}, bf16[1,256,4096]{2,1,0:T(8,128)(2,1)}, u32[]{:S(2)}) copy-start(bf16[1,256,4096]{2,1,0:T(8,128)(2,1)} %param.22) | copy-start | bytes 6291460
  6.5 117.8 %all-reduce.2.cloned.1.call-start = ((), (), s32[]{:S(2)}) async-start(), calls=%async_computation.1 | async-start | bytes 393216 | tf_op jit(solution)/shard_map/psum | solution.py:124
  10.0 193.8 %all-gather.3.cloned.1.call-start = ((), (), s32[]{:S(2)}) async-start(), calls=%async_computation.3 | async-start | bytes 4325376 | tf_op jit(solution)/shard_map/all_gather | solution.py:24
  139.7 5.3 %copy-start.4 = (bf16[4096]{0:T(1024)(128)(2,1)S(1)}, bf16[4096]{0:T(1024)(128)(2,1)}, u32[]{:S(2)}) copy-start(bf16[4096]{0:T(1024)(128)(2,1)} %param.17) | copy-start | bytes 24580
  139.7 5.3 %copy-start.3 = (s32[4,16,2]{1,2,0:T(2,128)S(1)}, s32[4,16,2]{1,2,0:T(2,128)}, u32[]{:S(2)}) copy-start(s32[4,16,2]{1,2,0:T(2,128)} %param.27) | copy-start | bytes 1540
  144.8 250.9 %reduce-scatter.2.cloned.1.call-start = ((), (), s32[]{:S(2)}) async-start(), calls=%async_computation.2 | async-start | bytes 405504 | tf_op jit(solution)/shard_map/reduce_scatter | solution.py:285
  209.4 50.4 %copy-start.1 = (bf16[512,128]{1,0:T(8,128)(2,1)S(1)}, bf16[512,128]{1,0:T(8,128)(2,1)}, u32[]{:S(2)}) copy-start(bf16[512,128]{1,0:T(8,128)(2,1)} %param.19) | copy-start | bytes 393220
  209.4 80.8 %copy-start.2 = (bf16[4,16,128]{2,1,0:T(8,128)(2,1)S(1)}, bf16[4,16,128]{2,1,0:T(8,128)(2,1)}, u32[]{:S(2)}) copy-start(bf16[4,16,128]{2,1,0:T(8,128)(2,1)} %param.15) | copy-start | bytes 49156
  313.4 6.6 %copy-start.5 = (bf16[4096,8]{0,1:T(8,128)(2,1)S(1)}, bf16[4096,8]{0,1:T(8,128)(2,1)}, u32[]{:S(2)}) copy-start(bf16[4096,8]{0,1:T(8,128)(2,1)} %param.20) | copy-start | bytes 196612
Sparse Core Ops, SparseCore 0:
  10.6 113.7 all-reduce.1
  144.9 49.8 all-gather.2
  317.7 77.8 reduce-scatter.1
where the time goes:
time: 435 us; the launch traced here: 434 us
  blocking collectives  192 us (44%)
  waiting for transfers between devices  96.8 us (22%)
  local copies, waits for them, and re-layouts  80.5 us (19%)
  other arithmetic  27.1 us (6%)
  matrix products  22.6 us (5%)
  between operations  13.7 us (3%)
    reduce_scatter x1, waiting for transfers between devices, body(): lax.psum_scatter(down_part, 'blk', scatter_dimension=1, tiled=True)  75.3 us
    psum x1, blocking collectives, body(): projected_rows, square_sum = lax.psum((partial_proj, partial_sq), 'blk')  62.3 us
    psum x2, blocking collectives, head_total(): return lax.psum(partial_value, 'kv')  60.4 us
    all_gather x2, blocking collectives, joined(): pieces = jax.tree.map(lambda part: lax.all_gather(part, axis), value)  46.7 us
    dynamic_slice x31, local copies, waits for them, and re-layouts, joined(): lax.scan(lambda running, section: (join(running, section), None), head, t...  28.3 us
    all_gather x1, blocking collectives, body(): full_rows = lax.all_gather(residual, 'blk', axis=1, tiled=True)  22.5 us
    psum x1, waiting for transfers between devices, body(): projected_rows, square_sum = lax.psum((partial_proj, partial_sq), 'blk')  21.4 us
    add x31, other arithmetic, combine_parts(): vector_one * scale_one[..., None] + vector_two * scale_two[..., None]  13.1 us
  transfers between devices with their start and end apart: 3, of which 2 were waited for; matrix products, arithmetic and copies ran while one was open for 10% of the time, Pallas kernels for 0%

commit v1 on v0

--- a/solution.py
+++ b/solution.py
@@ -263,7 +263,9 @@
     row_own = (row_start + jnp.arange(rows_local, dtype=jnp.int32)) // rows_per_expert
     in_flat = expert_in.reshape(experts_local, MODEL_WIDTH, 2 * ff_local)
     gain_wide = ffn_gain.astype(jnp.float32)
-    full_rows = lax.all_gather(residual, "blk", axis=1, tiled=True)
+    full_rows = jnp.concatenate(
+        lax.all_to_all(jnp.stack([residual] * lax.axis_size("blk")), "blk", 0, 0), axis=1
+    )
     chosen = full_rows[row_token].astype(jnp.float32)
     pre_rows = (chosen * gain_wide).astype(jnp.bfloat16)
     sums_in = jnp.einsum(

time: 435 us -> 422 us (0.970)
  blocking collectives: 192 us -> 170 us
  starting transfers between devices: 0.27 us -> 5.25 us
    all_gather x1 -> x0, blocking collectives: 22.5 us -> none  [body(): full_rows = lax.all_gather(residual, 'blk', axis=1, tiled=True)]
    all_to_all x0 -> x1, starting transfers between devices: none -> 5.17 us  [body(): lax.all_to_all(jnp.stack([residual] * lax.axis_size('blk')), 'blk', 0, 0)]
  transfers between devices with their start and end apart: 3 -> 4, of which waited for: 2 -> 3; matrix products, arithmetic and copies ran while one was open for 10% -> 11% of each run, Pallas kernels for 0% -> 0%
where the time goes in v1:
time: 422 us; the launch traced here: 421 us
  blocking collectives  170 us (40%)
  waiting for transfers between devices  99.7 us (24%)
  local copies, waits for them, and re-layouts  81.5 us (19%)
  other arithmetic  27.1 us (6%)
  matrix products  22.6 us (5%)
  between operations  13.7 us (3%)
  starting transfers between devices  5.25 us (1%)
    reduce_scatter x1, waiting for transfers between devices, body(): lax.psum_scatter(down_part, 'blk', scatter_dimension=1, tiled=True)  74.3 us
    psum x1, blocking collectives, body(): projected_rows, square_sum = lax.psum((partial_proj, partial_sq), 'blk')  62.4 us
    psum x2, blocking collectives, head_total(): return lax.psum(partial_value, 'kv')  60.5 us
    all_gather x2, blocking collectives, joined(): pieces = jax.tree.map(lambda part: lax.all_gather(part, axis), value)  47 us
    dynamic_slice x31, local copies, waits for them, and re-layouts, joined(): lax.scan(lambda running, section: (join(running, section), None), head, t...  28.3 us
    psum x1, waiting for transfers between devices, body(): projected_rows, square_sum = lax.psum((partial_proj, partial_sq), 'blk')  21.2 us
    add x31, other arithmetic, combine_parts(): vector_one * scale_one[..., None] + vector_two * scale_two[..., None]  13.1 us
  transfers between devices with their start and end apart: 4, of which 3 were waited for; matrix products, arithmetic and copies ran while one was open for 11% of the time, Pallas kernels for 0%

profile of v1, /device:TPU:2, one launch (start us, length us, event | category | flops | bytes accessed | tf_op | source)
XLA Modules:
  0.0 420.8 jit_solution(6033154783263802793)
XLA Ops:
  8.2 1.8 fusion.31
  10.0 1.3 fusion.108
  12.1 8.0 %scatter_custom_fusion = s32[2048]{0:T(1024)S(1)} fusion(s32[2048]{0:T(1024)S(1)} %bitcast.255, s32[2048]{0:T(1024)S(1)} %add_select_fusion, s32[]{:T(128)} %constant.125.clone.1), kind=kCustom, calls=%fused_computation.169 | custom fusion | bytes 8196 | tf_op jit(solution)/shard_map/scatter | solution.py:143
  20.1 8.0 %scatter_custom_fusion.1 = s32[2048]{0:T(1024)S(1)} fusion(s32[2048]{0:T(1024)S(1)} %bitcast.256, s32[2048]{0:T(1024)S(1)} %fusion.64, s32[]{:T(128)} %constant.125.clone.1), kind=kCustom, calls=%fused_computation.167 | custom fusion | bytes 8196 | tf_op jit(solution)/shard_map/scatter | solution.py:148
  28.2 1.3 fusion.86
  29.5 1.4 compare_select_fusion.12
  39.1 62.4 %psum.29 = f32[64]{0:T(128)S(1)} all-reduce(f32[64]{0:T(128)S(1)} %reduce_sum.66), channel_id=1, replica_groups=mesh['kv'=8,'blk'=32] {'blk'}, use_global_device_ids=true, to_apply=%region_4.5 | all-reduce | flops 64 | bytes 512 | tf_op jit(solution)/shard_map/psum | solution.py:124
  103.2 21.2 %all-reduce.2.cloned.1.call-done = f32[64,768]{1,0:T(8,128)} async-done(((f32[64,768]{1,0:T(8,128)}), f32[64,768]{1,0:T(8,128)}) %all-reduce.2.cloned.1.call-update) | async-done | bytes 196624 | tf_op jit(solution)/shard_map/psum | solution.py:124
  124.4 1.0 broadcast_multiply_fusion
  125.9 2.2 gather_fusion.11
  128.1 4.7 %fusion.8 = (f32[64,128]{1,0:T(8,128)S(1)}, f32[64,128,128]{1,2,0:T(8,128)}) fusion(pred[64,128]{1,0:T(8,128)(4,1)S(1)} %broadcast_compare_fusion.1, pred[64,128]{1,0:T(8,128)(4,1)S(1)} %add_compare_fusion, bf16[64,128,128]{2,1,0:T(8,128)(2,1)} %gather_fusion.11, bf16[64,2,1,128,128]{4,3,2,1,0:T(8,128)(2,1)} %param.23), kind=kOutput, calls=%fused_computation.35 | convolution fusion | flops 272621568 | bytes 8437760 | tf_op jit(solution)/shard_map/ptd,pqd->ptq/dot_general | solution.py:177
  134.0 5.8 %convolution_multiply_fusion = f32[64,128,128]{2,1,0:T(8,128)S(1)} fusion(f32[64,128,128]{1,2,0:T(8,128)} %get-tuple-element.131, f32[64,128]{1,0:T(8,128)S(1)} %subtract_exponential_fusion.1, bf16[64,2,1,128,128]{4,3,2,1,0:T(8,128)(2,1)} %param.23, f32[64,128]{1,0:T(8,128)S(1)} %get-tuple-element.130, pred[64,128]{1,0:T(8,128)(4,1)S(1)} %broadcast_compare_fusion.1, ...), kind=kOutput, calls=%fused_computation.38 | convolution fusion | flops 275775488 | bytes 10567680 | tf_op jit(solution)/shard_map/ptq,ptd->pqd/dot_general | solution.py:185
  139.9 3.8 fusion.6
  144.0 0.9 fusion.26
  146.0 3.8 fusion.10
  150.6 22.3 %all_gather.10 = f32[32,4,16,1,4]{2,4,3,1,0:T(4,128)S(1)} all-gather(f32[1,4,16,1,4]{2,4,3,1,0:T(4,128)S(1)} %get-tuple-element.113), channel_id=1, replica_groups=mesh['kv'=8,'blk'=32] {'blk'}, dimensions={0}, use_global_device_ids=true | all-gather | bytes 33792 | tf_op jit(solution)/shard_map/all_gather | solution.py:24
  172.9 24.6 %all_gather.9 = f32[32,4,16,1,4]{2,4,3,1,0:T(4,128)S(1)} all-gather(f32[1,4,16,1,4]{2,4,3,1,0:T(4,128)S(1)} %get-tuple-element.114), channel_id=1, replica_groups=mesh['kv'=8,'blk'=32] {'blk'}, dimensions={0}, use_global_device_ids=true | all-gather | bytes 33792 | tf_op jit(solution)/shard_map/all_gather | solution.py:24
  197.6 0.9 slice_bitcast_fusion.2
  198.6 4.6 %slice.137 = f32[124,16,4,128]{3,1,2,0:T(8,128)} slice(f32[128,16,4,128]{3,1,2,0:T(8,128)} %all-gather.3.cloned.1.call-done), slice={[4:128], [0:16], [0:4], [0:128]} | slice | bytes 8126464 | tf_op jit(solution)/shard_map/slice | solution.py:26
  203.2 50.2 %while.14 = (s32[]{:T(128)}, f32[4,16,1,4]{1,3,2,0:T(4,128)S(1)}, f32[4,16,1,4]{1,3,2,0:T(4,128)S(1)}, f32[4,16,1,4,128]{4,3,2,1,0:T(4,128)S(1)}, f32[31,4,16,1,...) while((s32[]{:T(128)}, f32[4,16,1,4]{1,3,2,0:T(4,128)S(1)}, ...), condition=%wide.region_11.12_spmd, body=%wide.region_10.11_spmd.sunk | while | flops 100098 | bytes 674921 | solution.py:27
  203.5 0.9 constant_dynamic-slice_fusion.2
  205.1 0.9 constant_dynamic-slice_fusion.2
  206.7 0.9 constant_dynamic-slice_fusion.2
  208.4 0.9 constant_dynamic-slice_fusion.2
  210.0 0.9 constant_dynamic-slice_fusion.2
  211.6 0.9 constant_dynamic-slice_fusion.2
  213.2 0.9 constant_dynamic-slice_fusion.2
  214.8 0.9 constant_dynamic-slice_fusion.2
  216.4 0.9 constant_dynamic-slice_fusion.2
  218.1 0.9 constant_dynamic-slice_fusion.2
  219.7 0.9 constant_dynamic-slice_fusion.2
  221.3 0.9 constant_dynamic-slice_fusion.2
  222.9 0.9 constant_dynamic-slice_fusion.2
  224.5 0.9 constant_dynamic-slice_fusion.2
  226.2 0.9 constant_dynamic-slice_fusion.2
  227.8 0.9 constant_dynamic-slice_fusion.2
  229.4 0.9 constant_dynamic-slice_fusion.2
  231.0 0.9 constant_dynamic-slice_fusion.2
  232.6 0.9 constant_dynamic-slice_fusion.2
  234.3 0.9 constant_dynamic-slice_fusion.2
  235.9 0.9 constant_dynamic-slice_fusion.2
  237.5 0.9 constant_dynamic-slice_fusion.2
  239.1 0.9 constant_dynamic-slice_fusion.2
  240.7 0.9 constant_dynamic-slice_fusion.2
  242.4 0.9 constant_dynamic-slice_fusion.2
  244.0 0.9 constant_dynamic-slice_fusion.2
  245.6 0.9 constant_dynamic-slice_fusion.2
  247.2 0.9 constant_dynamic-slice_fusion.2
  248.8 0.9 constant_dynamic-slice_fusion.2
  250.4 0.9 constant_dynamic-slice_fusion.2
  252.1 0.9 constant_dynamic-slice_fusion.2
  253.8 30.2 %psum.30 = f32[64,128]{1,0:T(8,128)S(1)} all-reduce(f32[64,128]{1,0:T(8,128)S(1)} %fusion.38), channel_id=1, replica_groups=mesh['kv'=8,'blk'=32] {'kv'}, use_global_device_ids=true, to_apply=%region_12.13 | all-reduce | flops 8192 | bytes 65536 | tf_op jit(solution)/shard_map/psum | solution.py:74
  284.1 0.9 stack.119
  285.0 5.2 %all-to-all-start = ((bf16[32,64,128]{2,1,0:T(8,128)(2,1)}), bf16[32,64,128]{2,1,0:T(8,128)(2,1)S(1)}, u32[]{:S(2)}, u32[]{:S(2)}) async-start(bf16[32,64,128]{2,1,0:T(8,128)(2,1)} %stack.119), calls=%async_computation | async-start | bytes 1048576 | tf_op jit(solution)/shard_map/all_to_all | solution.py:267
  290.5 4.9 %copy.156 = bf16[512,8,2,256]{3,1,2,0:T(8,128)(2,1)} copy(bf16[512,8,2,256]{3,2,1,0:T(2,128)(2,1)} %bitcast.238) | data formatting | bytes 8388608
  295.4 1.0 scatter_custom_fusion.2
  296.4 4.1 all-to-all-done
  301.4 2.8 fusion.28
  304.3 1.1 fusion.15
  305.8 1.0 scatter_custom_fusion.4
  306.9 1.0 scatter_custom_fusion.3
  308.2 74.3 %reduce-scatter.2.cloned.1.call-done = f32[24,128]{1,0:T(8,128)} async-done(((f32[24,4096]{1,0:T(8,128)}), f32[24,128]{1,0:T(8,128)}) %reduce-scatter.2.cloned.1.call-update) | async-done | bytes 12304 | tf_op jit(solution)/shard_map/reduce_scatter | solution.py:287
  382.5 0.9 fusion.59
  383.4 30.2 %psum.31 = f32[64,128]{1,0:T(8,128)S(1)} all-reduce(f32[64,128]{1,0:T(8,128)S(1)} %fusion.59), channel_id=1, replica_groups=mesh['kv'=8,'blk'=32] {'kv'}, use_global_device_ids=true, to_apply=%region_22.23 | all-reduce | flops 8192 | bytes 65536 | tf_op jit(solution)/shard_map/psum | solution.py:74
  (336 shorter events, 39.9 us)
Async XLA Ops:
  6.5 297.7 %copy-start = (bf16[1,256,4096]{2,1,0:T(8,128)(2,1)S(1)}, bf16[1,256,4096]{2,1,0:T(8,128)(2,1)}, u32[]{:S(2)}) copy-start(bf16[1,256,4096]{2,1,0:T(8,128)(2,1)} %param.22) | copy-start | bytes 6291460
  6.5 117.9 %all-reduce.2.cloned.1.call-start = ((), (), s32[]{:S(2)}) async-start(), calls=%async_computation.2 | async-start | bytes 393216 | tf_op jit(solution)/shard_map/psum | solution.py:124
  10.0 187.7 %all-gather.3.cloned.1.call-start = ((), (), s32[]{:S(2)}) async-start(), calls=%async_computation.4 | async-start | bytes 4325376 | tf_op jit(solution)/shard_map/all_gather | solution.py:24
  139.8 5.1 %copy-start.4 = (bf16[4096]{0:T(1024)(128)(2,1)S(1)}, bf16[4096]{0:T(1024)(128)(2,1)}, u32[]{:S(2)}) copy-start(bf16[4096]{0:T(1024)(128)(2,1)} %param.17) | copy-start | bytes 24580
  139.8 5.1 %copy-start.3 = (s32[4,16,2]{1,2,0:T(2,128)S(1)}, s32[4,16,2]{1,2,0:T(2,128)}, u32[]{:S(2)}) copy-start(s32[4,16,2]{1,2,0:T(2,128)} %param.27) | copy-start | bytes 1540
  203.2 50.4 %copy-start.1 = (bf16[512,128]{1,0:T(8,128)(2,1)S(1)}, bf16[512,128]{1,0:T(8,128)(2,1)}, u32[]{:S(2)}) copy-start(bf16[512,128]{1,0:T(8,128)(2,1)} %param.19) | copy-start | bytes 393220
  203.2 80.8 %copy-start.2 = (bf16[4,16,128]{2,1,0:T(8,128)(2,1)S(1)}, bf16[4,16,128]{2,1,0:T(8,128)(2,1)}, u32[]{:S(2)}) copy-start(bf16[4,16,128]{2,1,0:T(8,128)(2,1)} %param.15) | copy-start | bytes 49156
  285.0 15.6 %all-to-all-start = ((bf16[32,64,128]{2,1,0:T(8,128)(2,1)}), bf16[32,64,128]{2,1,0:T(8,128)(2,1)S(1)}, u32[]{:S(2)}, u32[]{:S(2)}) async-start(bf16[32,64,128]{2,1,0:T(8,128)(2,1)} %stack.119), calls=%async_computation | async-start | bytes 1048576 | tf_op jit(solution)/shard_map/all_to_all | solution.py:267
  290.1 92.4 %reduce-scatter.2.cloned.1.call-start = ((), (), s32[]{:S(2)}) async-start(), calls=%async_computation.3 | async-start | bytes 405504 | tf_op jit(solution)/shard_map/reduce_scatter | solution.py:287
  301.3 6.6 %copy-start.5 = (bf16[4096,8]{0,1:T(8,128)(2,1)S(1)}, bf16[4096,8]{0,1:T(8,128)(2,1)}, u32[]{:S(2)}) copy-start(bf16[4096,8]{0,1:T(8,128)(2,1)} %param.20) | copy-start | bytes 196612
Sparse Core Ops, SparseCore 0:
  10.6 113.7 all-reduce.1
  145.0 49.9 all-gather.2
  305.6 76.8 reduce-scatter.1
